TPU v7x, 512 devices: a whole 4x4x16 slice. The times are simulated.
512 devices in a mesh: row: 32 (over x, z_hi, core), col: 16 (over z_lo, y).
Axes of the slice: x: 4, y: 4, z: 16 (z_hi: 4, z_lo: 4; z = z_hi * 4 + z_lo), core: 2. Of those that a mesh axis runs over, the one named last changes fastest.
Arguments:
- images: bfloat16 [32, 128, 128, 256], P('row', 'col'), may hold values from -6 to 6
- weight: bfloat16 [3, 3, 256, 256], P(None, None, None, 'col'), may hold values from -0.125 to 0.125
- norm_gain: float32 [256], replicated, may hold values from 0.5 to 1.5
- cotangent: bfloat16 [32, 128, 128, 256], P('row', 'col'), may hold values from -6 to 6
Outputs:
- features: bfloat16 [32, 128, 128, 256], P('row', 'col')
- input_grad: bfloat16 [32, 128, 128, 256], P('row', 'col')
- weight_grad: float32 [3, 3, 256, 256], P(None, None, None, 'col')
All inputs are finite; a program needn't handle non-finite values.
Results may differ from a plain program's by a relative error of at most 0.013.
Values may be sent and summed in bfloat16 or wider, within the bound.
No kernel may reach another device: no remote copies, remote signals or barrier semaphores. Data moves between devices by JAX's collectives and lax.ppermute only.
A program may use at most 64 MiB of HBM per device.

v0:
```python
import math
import jax
import jax.numpy as jnp
from jax import lax
from jax.sharding import PartitionSpec as P

epsilon = 1e-06
root_half = 0.7071067811865476
norm_const = 0.3989422804014327


def padded_2(value, sides, width):
    for axis, dim in sides:
        peers, length = (lax.axis_size(axis), value.shape[dim])
        up = [(i, (i + 1) % peers) for i in range(peers - 1)]
        down = [(j, i) for i, j in up]
        last = lax.slice_in_dim(value, length - width, length, axis=dim)
        initial = lax.slice_in_dim(value, 0, width, axis=dim)
        before = lax.ppermute(last, axis, up)
        after = lax.ppermute(initial, axis, down)
        value = jnp.concatenate([before, value, after], axis=dim)
    return value


def norm_act(conv_out, upper, norm_gain):
    mean_val = jnp.mean(conv_out, axis=-1, keepdims=True)
    centred = conv_out - mean_val
    variance = jnp.mean(centred * centred, axis=-1, keepdims=True)
    inv_std = lax.rsqrt(variance + epsilon)
    unit = centred * inv_std
    normed = unit * norm_gain
    cdf_val = 0.5 * (1.0 + lax.erf(normed * root_half))
    density = jnp.exp(-0.5 * normed * normed) * norm_const
    outputs = (normed * cdf_val).astype(jnp.bfloat16)
    upstream = upper.astype(jnp.float32) * (cdf_val + normed * density) * norm_gain
    mean_up = jnp.mean(upstream, axis=-1, keepdims=True)
    mean_cross = jnp.mean(upstream * unit, axis=-1, keepdims=True)
    grad_pre = inv_std * (upstream - mean_up - unit * mean_cross)
    return (outputs, grad_pre.astype(jnp.bfloat16))


def window(padded, tap_row, tap_col, tile_rows, tile_cols):
    return padded[:, tap_row : tap_row + tile_rows, tap_col : tap_col + tile_cols, :].reshape(
        -1, padded.shape[-1]
    )


def on_device(images, weight, norm_gain, cotangent):
    img_count, tile_rows, tile_cols, in_chan = images.shape
    whole_kernel = lax.all_gather(weight, "col", axis=3, tiled=True)
    out_chan = whole_kernel.shape[3]
    rimmed = padded_2(images, (("col", 1),), 1)
    padded = jnp.pad(rimmed, ((0, 0), (0, 0), (1, 1), (0, 0)))
    conv_out = jnp.zeros((img_count * tile_rows * tile_cols, out_chan), jnp.float32)
    for tap_row in range(3):
        for tap_col in range(3):
            conv_out = conv_out + jnp.dot(
                window(padded, tap_row, tap_col, tile_rows, tile_cols),
                whole_kernel[tap_row, tap_col],
                preferred_element_type=jnp.float32,
            )
    outputs, grad_pre = norm_act(conv_out, cotangent.reshape(-1, out_chan), norm_gain)
    grad_grid = grad_pre.reshape(img_count, tile_rows, tile_cols, out_chan)
    grad_rimmed = padded_2(grad_grid, (("col", 1),), 1)
    grad_pad = jnp.pad(grad_rimmed, ((0, 0), (0, 0), (1, 1), (0, 0)))
    grad_input = jnp.zeros((img_count * tile_rows * tile_cols, in_chan), jnp.float32)
    pieces = []
    for tap_row in range(3):
        for tap_col in range(3):
            grad_input = grad_input + lax.dot_general(
                window(grad_pad, 2 - tap_row, 2 - tap_col, tile_rows, tile_cols),
                whole_kernel[tap_row, tap_col],
                (((1,), (1,)), ((), ())),
                preferred_element_type=jnp.float32,
            )
            pieces.append(
                lax.dot_general(
                    window(padded, tap_row, tap_col, tile_rows, tile_cols),
                    grad_pre,
                    (((0,), (0,)), ((), ())),
                    preferred_element_type=jnp.float32,
                )
            )
    partial_value = jnp.stack(pieces).reshape(3, 3, in_chan, out_chan)
    col_sum = lax.psum_scatter(partial_value, "col", scatter_dimension=3, tiled=True)
    own_share = lax.psum(col_sum, "row")
    pixels = img_count * lax.axis_size("row") * tile_rows * lax.axis_size("col") * tile_cols
    weight_grad = own_share * (1.0 / math.sqrt(pixels))
    features = outputs.reshape(img_count, tile_rows, tile_cols, out_chan)
    input_grad = grad_input.astype(jnp.bfloat16).reshape(img_count, tile_rows, tile_cols, in_chan)
    return (features, input_grad, weight_grad)


def solution(mesh):
    placed = (
        P("row", "col", None, None),
        P(None, None, None, "col"),
        P(),
        P("row", "col", None, None),
    )
    return jax.shard_map(
        on_device,
        mesh=mesh,
        in_specs=placed,
        out_specs=(
            P("row", "col", None, None),
            P("row", "col", None, None),
            P(None, None, None, "col"),
        ),
        check_vma=False,
    )
```

profile of v0, /device:TPU:1, one launch (start us, length us, event | category | flops | bytes accessed | tf_op | source)
XLA Modules:
  0.0 546.5 jit_solution(15703114254889258676)
XLA Ops:
  8.8 4.0 collective-permute-start
  12.9 1.3 collective-permute-start.1
  14.2 3.7 collective-permute-done.1
  17.9 1.2 select_maximum_fusion.2
  20.2 1.4 fusion.27
  21.5 70.6 %all-gather.2.cloned.1.call-done = bf16[3,3,256,256]{2,3,1,0:T(8,128)(2,1)} async-done(((bf16[3,3,256,16]{2,3,1,0:T(8,128)(2,1)}), bf16[3,3,256,256]{2,3,1,0:T(8,128)(2,1)}) %all-gather.2.cloned.1.call-update) | async-done | bytes 1179664 | tf_op jit(solution)/shard_map/all_gather | solution.py:50
  92.2 1.4 fusion.21
  99.6 1.9 fusion.24
  102.3 1.0 fusion.12
  103.4 1.1 fusion.11
  104.4 1.1 fusion.10
  105.5 1.0 fusion.9
  106.5 1.0 fusion.8
  107.6 1.1 fusion.7
  109.6 1.0 fusion.5
  110.7 1.0 fusion.4
  111.7 3.1 copy.8
  115.0 2.7 collective-permute-start.2
  117.7 1.3 collective-permute-start.3
  119.0 3.7 collective-permute-done.3
  126.6 79.9 %reduce-scatter.2.cloned.1.call-done = f32[3,3,256,16]{2,3,1,0:T(8,128)} async-done(((f32[3,3,256,256]{2,3,1,0:T(8,128)}), f32[3,3,256,16]{2,3,1,0:T(8,128)}) %reduce-scatter.2.cloned.1.call-update) | async-done | bytes 147472 | tf_op jit(solution)/shard_map/reduce_scatter | solution.py:85
  206.6 2.1 fusion.3
  208.7 329.7 %all-reduce.4.cloned.1.call-done = f32[3,3,256,16]{2,3,1,0:T(8,128)} async-done(((f32[3,3,256,16]{2,3,1,0:T(8,128)}), f32[3,3,256,16]{2,3,1,0:T(8,128)}) %all-reduce.4.cloned.1.call-update) | async-done | bytes 147472 | tf_op jit(solution)/shard_map/psum | solution.py:86
  538.4 1.6 broadcast_multiply_fusion
  (58 shorter events, 14.4 us)
Async XLA Ops:
  7.2 12.0 %copy-start = (bf16[1,8,128,256]{3,2,1,0:T(8,128)(2,1)S(1)}, bf16[1,8,128,256]{3,2,1,0:T(8,128)(2,1)}, u32[]{:S(2)}) copy-start(bf16[1,8,128,256]{3,2,1,0:T(8,128)(2,1)} %param.4) | copy-start | bytes 1572868
  7.2 85.0 %all-gather.2.cloned.1.call-start = ((), (), s32[]{:S(2)}) async-start(), calls=%async_computation.1 | async-start | bytes 1253376 | tf_op jit(solution)/shard_map/all_gather | solution.py:50
  7.9 198.6 %reduce-scatter.2.cloned.1.call-start = ((), (), s32[]{:S(2)}) async-start(), calls=%async_computation.2 | async-start | bytes 2506752 | tf_op jit(solution)/shard_map/reduce_scatter | solution.py:85
  8.8 5.4 collective-permute-start
  12.9 5.0 collective-permute-start.1
  21.5 75.5 %copy-start.2 = (bf16[1,8,128,256]{3,2,1,0:T(8,128)(2,1)}, bf16[1,8,128,256]{3,2,1,0:T(8,128)(2,1)S(1)}, u32[]{:S(2)}) copy-start(bf16[1,8,128,256]{3,2,1,0:T(8,128)(2,1)S(1)} %get-tuple-element.13) | copy-start | bytes 1572868
  92.2 1.4 copy-start.1
  92.2 1.7 copy-start.8
  93.9 1.0 copy-start.6
  94.2 1.1 copy-start.5
  95.7 1.0 copy-start.4
  97.0 1.0 copy-start.7
  98.1 0.8 copy-start.10
  98.5 1.0 copy-start.9
  106.5 2.1 copy-start.3
  114.9 423.5 %all-reduce.4.cloned.1.call-start = ((), (), s32[]{:S(2)}) async-start(), calls=%async_computation.3 | async-start | bytes 294912 | tf_op jit(solution)/shard_map/psum | solution.py:86
  115.0 4.1 collective-permute-start.2
  117.7 5.0 collective-permute-start.3
Sparse Core Ops, SparseCore 0:
  10.1 82.0 all-gather.1
  115.0 91.4 reduce-scatter.1
  209.5 328.8 all-reduce.3
where the time goes:
time: 547 us
  waiting for transfers between devices  488 us (89%)
  matrix products  18 us (3%)
  between operations  14 us (3%)
  starting transfers between devices  9.47 us (2%)
  local copies, waits for them, and re-layouts  8.58 us (2%)
  other arithmetic  8.02 us (1%)
    psum x1, waiting for transfers between devices, on_device(): own_share = lax.psum(col_sum, 'row')  330 us
    reduce_scatter x1, waiting for transfers between devices, on_device(): lax.psum_scatter(partial_value, 'col', scatter_dimension=3, tiled=True)  79.9 us
    all_gather x1, waiting for transfers between devices, on_device(): whole_kernel = lax.all_gather(weight, 'col', axis=3, tiled=True)  70.6 us
  transfers between devices with their start and end apart: 7, of which 5 were waited for; matrix products, arithmetic and copies ran while one was open for 2% of the time, Pallas kernels for 0%

commit v1 on v0

--- a/solution.py
+++ b/solution.py
@@ -7,6 +7,9 @@
 epsilon = 1e-06
 root_half = 0.7071067811865476
 norm_const = 0.3989422804014327
+plan_the_lanes = lambda block_in, link_axis: jnp.concatenate(
+    lax.all_to_all(jnp.stack(lax.axis_size(link_axis) * [block_in]), link_axis, 0, 0), 3
+)
 
 
 def padded_2(value, sides, width):
@@ -47,7 +50,7 @@
 
 def on_device(images, weight, norm_gain, cotangent):
     img_count, tile_rows, tile_cols, in_chan = images.shape
-    whole_kernel = lax.all_gather(weight, "col", axis=3, tiled=True)
+    whole_kernel = plan_the_lanes(weight, "col")
     out_chan = whole_kernel.shape[3]
     rimmed = padded_2(images, (("col", 1),), 1)
     padded = jnp.pad(rimmed, ((0, 0), (0, 0), (1, 1), (0, 0)))

time: 547 us -> 499 us (0.912)
  waiting for transfers between devices: 488 us -> 432 us
  starting transfers between devices: 9.47 us -> 17.2 us
    all_gather x1 -> x0, waiting for transfers between devices: 70.6 us -> none  [on_device(): whole_kernel = lax.all_gather(weight, 'col', axis=3, tiled=True)]
    all_to_all x0 -> x1, waiting for transfers between devices: none -> 12.5 us  [lax.all_to_all(jnp.stack(lax.axis_size(link_axis) * [block_in]), link_axi...]
    all_to_all x0 -> x1, starting transfers between devices: none -> 9.32 us  [lax.all_to_all(jnp.stack(lax.axis_size(link_axis) * [block_in]), link_axi...]
  transfers between devices with their start and end apart: 7 -> 7, of which waited for: 5 -> 6; matrix products, arithmetic and copies ran while one was open for 2% -> 2% of each run, Pallas kernels for 0% -> 0%
where the time goes in v1:
time: 499 us
  waiting for transfers between devices  432 us (87%)
  starting transfers between devices  17.2 us (3%)
  matrix products  17 us (3%)
  between operations  14.3 us (3%)
  local copies, waits for them, and re-layouts  11.3 us (2%)
  other arithmetic  7.06 us (1%)
    psum x1, waiting for transfers between devices, on_device(): own_share = lax.psum(col_sum, 'row')  330 us
    reduce_scatter x1, waiting for transfers between devices, on_device(): lax.psum_scatter(partial_value, 'col', scatter_dimension=3, tiled=True)  79.7 us
    all_to_all x1, waiting for transfers between devices, lax.all_to_all(jnp.stack(lax.axis_size(link_axis) * [block_in]), link_axi...  12.5 us
  transfers between devices with their start and end apart: 7, of which 6 were waited for; matrix products, arithmetic and copies ran while one was open for 2% of the time, Pallas kernels for 0%

profile of v1, /device:TPU:1, one launch (start us, length us, event | category | flops | bytes accessed | tf_op | source)
XLA Modules:
  0.0 498.7 jit_solution(3519851480546744558)
XLA Ops:
  7.2 2.0 stack.22
  9.2 9.3 %all-to-all-start = ((bf16[16,3,3,256,16]{3,4,2,1,0:T(8,128)(2,1)}), bf16[16,3,3,256,16]{3,4,2,1,0:T(8,128)(2,1)S(1)}, u32[]{:S(2)}, u32[]{:S(2)}) async-start(bf16[16,3,3,256,16]{3,4,2,1,0:T(8,128)(2,1)} %stack.22), calls=%async_computation | async-start | bytes 2359296 | tf_op jit(solution)/shard_map/all_to_all | solution.py:11
  18.6 3.3 collective-permute-start
  21.8 1.3 collective-permute-start.1
  23.1 1.2 collective-permute-done
  24.4 3.0 collective-permute-done.1
  27.5 1.1 pad_maximum_fusion.2
  28.6 1.6 fusion.27
  30.3 12.5 %all-to-all-done = bf16[16,3,3,256,16]{3,4,2,1,0:T(8,128)(2,1)S(1)} async-done(((bf16[16,3,3,256,16]{3,4,2,1,0:T(8,128)(2,1)}), bf16[16,3,3,256,16]{3,4,2,1,0:T(8,128)(2,1)S(1)}, u32[]{:S(2)}, u32[]{:S(2)}) %all-to-all-start) | async-done | bytes 1179680 | tf_op jit(solution)/shard_map/all_to_all | solution.py:11
  50.5 1.9 fusion.24
  53.3 1.0 fusion.12
  54.3 1.0 fusion.11
  55.4 1.1 fusion.10
  56.4 1.0 fusion.9
  57.5 1.1 fusion.8
  58.5 1.1 fusion.7
  62.7 3.1 copy.14
  65.9 1.9 collective-permute-start.2
  67.8 1.3 collective-permute-start.3
  69.1 5.7 %collective-permute-done.3 = bf16[1,1,128,256]{3,2,1,0:T(8,128)(2,1)S(1)} collective-permute-done((bf16[1,1,128,256]{3,2,1,0:T(8,128)(2,1)S(1)}, bf16[1,1,128,256]{3,2,1,0:T(8,128)(2,1)S(1)}, u32[]{:S(2)}, u32[]{:S(2)}) %collective-permute-start.3) | collective-permute-done | bytes 65568 | tf_op jit(solution)/shard_map/ppermute | solution.py:23
  78.8 79.7 %reduce-scatter.2.cloned.1.call-done = f32[3,3,256,16]{2,3,1,0:T(8,128)} async-done(((f32[3,3,256,256]{2,3,1,0:T(8,128)}), f32[3,3,256,16]{2,3,1,0:T(8,128)}) %reduce-scatter.2.cloned.1.call-update) | async-done | bytes 147472 | tf_op jit(solution)/shard_map/reduce_scatter | solution.py:88
  158.5 2.1 fusion.3
  160.7 329.6 %all-reduce.4.cloned.1.call-done = f32[3,3,256,16]{2,3,1,0:T(8,128)} async-done(((f32[3,3,256,16]{2,3,1,0:T(8,128)}), f32[3,3,256,16]{2,3,1,0:T(8,128)}) %all-reduce.4.cloned.1.call-update) | async-done | bytes 147472 | tf_op jit(solution)/shard_map/psum | solution.py:89
  490.3 1.6 broadcast_multiply_fusion
  (57 shorter events, 15.8 us)
Async XLA Ops:
  9.2 9.4 %copy-start = (bf16[1,8,128,256]{3,2,1,0:T(8,128)(2,1)S(1)}, bf16[1,8,128,256]{3,2,1,0:T(8,128)(2,1)}, u32[]{:S(2)}) copy-start(bf16[1,8,128,256]{3,2,1,0:T(8,128)(2,1)} %param.4) | copy-start | bytes 1572868
  9.2 33.6 %all-to-all-start = ((bf16[16,3,3,256,16]{3,4,2,1,0:T(8,128)(2,1)}), bf16[16,3,3,256,16]{3,4,2,1,0:T(8,128)(2,1)S(1)}, u32[]{:S(2)}, u32[]{:S(2)}) async-start(bf16[16,3,3,256,16]{3,4,2,1,0:T(8,128)(2,1)} %stack.22), calls=%async_computation | async-start | bytes 2359296 | tf_op jit(solution)/shard_map/all_to_all | solution.py:11
  18.5 140.0 %reduce-scatter.2.cloned.1.call-start = ((), (), s32[]{:S(2)}) async-start(), calls=%async_computation.2 | async-start | bytes 2506752 | tf_op jit(solution)/shard_map/reduce_scatter | solution.py:88
  18.6 5.8 %collective-permute-start = (bf16[1,1,128,256]{3,2,1,0:T(8,128)(2,1)S(1)}, bf16[1,1,128,256]{3,2,1,0:T(8,128)(2,1)S(1)}, u32[]{:S(2)}, u32[]{:S(2)}) collective-permute-start(bf16[1,1,128,256]{3,2,1,0:T(8,128)(2,1)S(1)} %get-tuple-element.25), channel_id=1, source_target_pairs={{0,1},{1,2},{2,3},{3,4},{4,5},{5,6},{6,7},{7,8},{8,9},{9,10},{10,1... | collective-permute-start | bytes 196616 | tf_op jit(solution)/shard_map/ppermute | solution.py:22
  21.8 5.5 %collective-permute-start.1 = (bf16[1,1,128,256]{3,2,1,0:T(8,128)(2,1)S(1)}, bf16[1,1,128,256]{3,2,1,0:T(8,128)(2,1)S(1)}, u32[]{:S(2)}, u32[]{:S(2)}) collective-permute-start(bf16[1,1,128,256]{3,2,1,0:T(8,128)(2,1)S(1)} %get-tuple-element.26), channel_id=1, source_target_pairs={{1,0},{2,1},{3,2},{4,3},{5,4},{6,5},{7,6},{8,7},{9,8},{10,9},{11,1... | collective-permute-start | bytes 196616 | tf_op jit(solution)/shard_map/ppermute | solution.py:23
  42.7 1.0 copy-start.1
  43.8 1.0 copy-start.7
  44.5 1.1 copy-start.5
  45.2 1.1 copy-start.4
  46.6 1.0 copy-start.3
  46.9 1.1 copy-start.2
  47.9 1.1 copy-start.6
  49.0 0.8 copy-start.9
  49.4 1.0 copy-start.8
  65.8 424.5 %all-reduce.4.cloned.1.call-start = ((), (), s32[]{:S(2)}) async-start(), calls=%async_computation.3 | async-start | bytes 294912 | tf_op jit(solution)/shard_map/psum | solution.py:89
  65.9 3.3 collective-permute-start.2
  67.8 7.1 %collective-permute-start.3 = (bf16[1,1,128,256]{3,2,1,0:T(8,128)(2,1)S(1)}, bf16[1,1,128,256]{3,2,1,0:T(8,128)(2,1)S(1)}, u32[]{:S(2)}, u32[]{:S(2)}) collective-permute-start(bf16[1,1,128,256]{3,2,1,0:T(8,128)(2,1)S(1)} %get-tuple-element.22), channel_id=1, source_target_pairs={{1,0},{2,1},{3,2},{4,3},{5,4},{6,5},{7,6},{8,7},{9,8},{10,9},{11,1... | collective-permute-start | bytes 196616 | tf_op jit(solution)/shard_map/ppermute | solution.py:23
Sparse Core Ops, SparseCore 0:
  65.9 92.5 reduce-scatter.1
  161.4 328.8 all-reduce.3

commit v2 on v0

--- a/solution.py
+++ b/solution.py
@@ -83,7 +83,8 @@
             )
     partial_value = jnp.stack(pieces).reshape(3, 3, in_chan, out_chan)
     col_sum = lax.psum_scatter(partial_value, "col", scatter_dimension=3, tiled=True)
-    own_share = lax.psum(col_sum, "row")
+    parts = lax.all_gather(col_sum, "row", axis=0, tiled=False)
+    own_share = parts.sum(axis=0)
     pixels = img_count * lax.axis_size("row") * tile_rows * lax.axis_size("col") * tile_cols
     weight_grad = own_share * (1.0 / math.sqrt(pixels))
     features = outputs.reshape(img_count, tile_rows, tile_cols, out_chan)

time: 547 us -> 422 us (0.77)
  waiting for transfers between devices: 488 us -> 357 us
  local copies, waits for them, and re-layouts: 8.58 us -> 14.3 us
    psum x1 -> x0, waiting for transfers between devices: 330 us -> none  [on_device(): own_share = lax.psum(col_sum, 'row')]
    unnamed x3 -> x4, waiting for transfers between devices: 0.71 us -> 181 us
    all_gather x0 -> x1, waiting for transfers between devices: none -> 97.9 us  [on_device(): parts = lax.all_gather(col_sum, 'row', axis=0, tiled=False)]
    reduce_scatter x1 -> x0, waiting for transfers between devices: 79.9 us -> none  [on_device(): lax.psum_scatter(partial_value, 'col', scatter_dimension=3, tiled=True)]
  transfers between devices with their start and end apart: 7 -> 7, of which waited for: 5 -> 6; matrix products, arithmetic and copies ran while one was open for 2% -> 2% of each run, Pallas kernels for 0% -> 0%
where the time goes in v2:
time: 422 us; the launch traced here: 421 us
  waiting for transfers between devices  357 us (85%)
  matrix products  17 us (4%)
  between operations  14.7 us (3%)
  local copies, waits for them, and re-layouts  14.3 us (3%)
  starting transfers between devices  9.56 us (2%)
  other arithmetic  8.47 us (2%)
    unnamed x4, waiting for transfers between devices  181 us
    all_gather x1, waiting for transfers between devices, on_device(): parts = lax.all_gather(col_sum, 'row', axis=0, tiled=False)  97.9 us
    all_gather x1, waiting for transfers between devices, on_device(): whole_kernel = lax.all_gather(weight, 'col', axis=3, tiled=True)  70.7 us
    dot_general x9, matrix products, on_device(): lax.dot_general(window(padded, tap_row, tap_col, tile_rows, tile_cols), g...  9.41 us
  transfers between devices with their start and end apart: 7, of which 6 were waited for; matrix products, arithmetic and copies ran while one was open for 2% of the time, Pallas kernels for 0%

profile of v2, /device:TPU:1, one launch (start us, length us, event | category | flops | bytes accessed | tf_op | source)
XLA Modules:
  0.0 421.2 jit_solution(3017448570923510313)
XLA Ops:
  8.8 4.0 collective-permute-start
  12.9 1.3 collective-permute-start.1
  14.2 3.7 collective-permute-done.1
  17.9 1.2 select_maximum_fusion.2
  20.2 1.4 fusion.27
  21.5 70.7 %all-gather.4.cloned.1.call-done = bf16[3,3,256,256]{2,3,1,0:T(8,128)(2,1)} async-done(((bf16[3,3,256,16]{2,3,1,0:T(8,128)(2,1)}), bf16[3,3,256,256]{2,3,1,0:T(8,128)(2,1)}) %all-gather.4.cloned.1.call-update) | async-done | bytes 1179664 | tf_op jit(solution)/shard_map/all_gather | solution.py:50
  92.2 1.4 fusion.21
  99.6 1.9 fusion.24
  102.3 1.0 fusion.12
  104.4 1.0 fusion.10
  106.5 1.1 fusion.8
  107.5 1.0 fusion.7
  108.6 1.1 fusion.6
  109.7 1.0 fusion.5
  110.7 1.1 fusion.4
  111.8 4.6 %copy.9 = f32[3,3,256,256]{2,1,0,3:T(4,128)} copy(f32[3,3,256,256]{3,2,1,0:T(8,128)} %bitcast.40) | data formatting | bytes 4718592 | tf_op jit(solution)/shard_map/reshape | solution.py:84
  116.4 1.3 dynamic-slice
  118.3 180.5 %all-reduce.5.cloned.1.call-done = f32[3,3,256,256]{2,1,0,3:T(4,128)} async-done(((f32[3,3,256,256]{2,1,0,3:T(4,128)}), f32[3,3,256,256]{2,1,0,3:T(4,128)}) %all-reduce.5.cloned.1.call-update) | async-done | bytes 2359312
  300.5 2.8 collective-permute-start.2
  303.4 1.3 collective-permute-start.3
  304.9 3.5 collective-permute-done.3
  311.5 1.1 fusion.3
  312.6 97.9 %all-gather.6.cloned.1.call-done = f32[96,3,256,16]{2,3,1,0:T(8,128)} async-done(((f32[3,3,256,16]{2,3,1,0:T(8,128)}), f32[96,3,256,16]{2,3,1,0:T(8,128)}) %all-gather.6.cloned.1.call-update) | async-done | bytes 4718608 | tf_op jit(solution)/shard_map/all_gather | solution.py:86
  410.5 2.7 reduce_sum.49
  (64 shorter events, 18.0 us)
Async XLA Ops:
  7.2 12.0 %copy-start = (bf16[1,8,128,256]{3,2,1,0:T(8,128)(2,1)S(1)}, bf16[1,8,128,256]{3,2,1,0:T(8,128)(2,1)}, u32[]{:S(2)}) copy-start(bf16[1,8,128,256]{3,2,1,0:T(8,128)(2,1)} %param.4) | copy-start | bytes 1572868
  7.2 85.0 %all-gather.4.cloned.1.call-start = ((), (), s32[]{:S(2)}) async-start(), calls=%async_computation | async-start | bytes 1253376 | tf_op jit(solution)/shard_map/all_gather | solution.py:50
  7.9 290.9 %all-reduce.5.cloned.1.call-start = ((), (), s32[]{:S(2)}) async-start(), calls=%async_computation.2 | async-start | bytes 6291456
  8.8 5.4 %collective-permute-start = (bf16[1,1,128,256]{3,2,1,0:T(8,128)(2,1)S(1)}, bf16[1,1,128,256]{3,2,1,0:T(8,128)(2,1)S(1)}, u32[]{:S(2)}, u32[]{:S(2)}) collective-permute-start(bf16[1,1,128,256]{3,2,1,0:T(8,128)(2,1)S(1)} %get-tuple-element.28), channel_id=1, source_target_pairs={{0,1},{1,2},{2,3},{3,4},{4,5},{5,6},{6,7},{7,8},{8,9},{9,10},{10,1... | collective-permute-start | bytes 196616 | tf_op jit(solution)/shard_map/ppermute | solution.py:19
  12.9 5.0 %collective-permute-start.1 = (bf16[1,1,128,256]{3,2,1,0:T(8,128)(2,1)S(1)}, bf16[1,1,128,256]{3,2,1,0:T(8,128)(2,1)S(1)}, u32[]{:S(2)}, u32[]{:S(2)}) collective-permute-start(bf16[1,1,128,256]{3,2,1,0:T(8,128)(2,1)S(1)} %get-tuple-element.29), channel_id=1, source_target_pairs={{1,0},{2,1},{3,2},{4,3},{5,4},{6,5},{7,6},{8,7},{9,8},{10,9},{11,1... | collective-permute-start | bytes 196616 | tf_op jit(solution)/shard_map/ppermute | solution.py:20
  21.5 75.5 %copy-start.2 = (bf16[1,8,128,256]{3,2,1,0:T(8,128)(2,1)}, bf16[1,8,128,256]{3,2,1,0:T(8,128)(2,1)S(1)}, u32[]{:S(2)}) copy-start(bf16[1,8,128,256]{3,2,1,0:T(8,128)(2,1)S(1)} %get-tuple-element.16) | copy-start | bytes 1572868
  92.2 1.4 copy-start.1
  92.2 1.7 copy-start.8
  93.9 1.0 copy-start.6
  94.2 1.1 copy-start.5
  95.7 1.0 copy-start.4
  97.0 1.0 copy-start.7
  98.1 0.8 copy-start.10
  98.5 1.0 copy-start.9
  106.5 2.1 copy-start.3
  116.3 294.1 %all-gather.6.cloned.1.call-start = ((), (), s32[]{:S(2)}) async-start(), calls=%async_computation.1 | async-start | bytes 4866048 | tf_op jit(solution)/shard_map/all_gather | solution.py:86
  300.5 4.4 %collective-permute-start.2 = (bf16[1,1,128,256]{3,2,1,0:T(8,128)(2,1)S(1)}, bf16[1,1,128,256]{3,2,1,0:T(8,128)(2,1)S(1)}, u32[]{:S(2)}, u32[]{:S(2)}) collective-permute-start(bf16[1,1,128,256]{3,2,1,0:T(8,128)(2,1)S(1)} %get-tuple-element.24), channel_id=1, source_target_pairs={{0,1},{1,2},{2,3},{3,4},{4,5},{5,6},{6,7},{7,8},{8,9},{9,10},{10,1... | collective-permute-start | bytes 196616 | tf_op jit(solution)/shard_map/ppermute | solution.py:19
  303.4 5.0 %collective-permute-start.3 = (bf16[1,1,128,256]{3,2,1,0:T(8,128)(2,1)S(1)}, bf16[1,1,128,256]{3,2,1,0:T(8,128)(2,1)S(1)}, u32[]{:S(2)}, u32[]{:S(2)}) collective-permute-start(bf16[1,1,128,256]{3,2,1,0:T(8,128)(2,1)S(1)} %get-tuple-element.25), channel_id=1, source_target_pairs={{1,0},{2,1},{3,2},{4,3},{5,4},{6,5},{7,6},{8,7},{9,8},{10,9},{11,1... | collective-permute-start | bytes 196616 | tf_op jit(solution)/shard_map/ppermute | solution.py:20
Sparse Core Ops, SparseCore 0:
  10.1 82.0 all-gather.3
  116.5 182.3 all-reduce.4
  302.5 107.8 all-gather.5
